TPU v7x, 32 devices: a whole 2x2x4 slice. The times are simulated.
32 devices in a mesh: ctx: 16 (over z, y, core), head: 2 (over x).
Axes of the slice: x: 2, y: 2, z: 4, core: 2. Of those that a mesh axis runs over, the one named last changes fastest.
Arguments:
- queries: bfloat16 [2048, 1536], P('ctx', 'head'), may hold values from -45 to 45
- key_rows: bfloat16 [2048, 256], P('ctx', 'head'), may hold values from -5 to 5
- value_rows: bfloat16 [2048, 256], P('ctx', 'head'), may hold values from -18 to 18
- cotangent: bfloat16 [2048, 1536], P('ctx', 'head'), may hold values from -6 to 6
- trace_ids: int32 [2048], P('ctx'), may hold values from 0 to 15, never falling along the last dimension, each value on 1 to 512 neighbouring positions
- correct: int32 [16], replicated, may hold values from 0 to 16, as said below
- group_size: int32 [16], replicated, may hold values from 4 to 16
Outputs:
- log_totals: float32 [2048, 12], P('ctx', 'head')
- grad_queries: float32 [2048, 1536], P('ctx', 'head')
- grad_keys: bfloat16 [2048, 256], P('ctx', 'head')
- grad_values: bfloat16 [2048, 256], P('ctx', 'head')
Inputs may be any that keep to these rules, and one draw needn't show every extreme that they name: correct[g] is at most group_size[g].
All inputs are finite; a program needn't handle non-finite values.
Results may differ from a plain program's by a relative error of at most 0.0054.
Values may be sent and summed in bfloat16 or wider, within the bound.
No kernel may reach another device: no remote copies, remote signals or barrier semaphores. Data moves between devices by JAX's collectives and lax.ppermute only.
A program may use at most 64 MiB of HBM per device.

v0:
```python
import math
import jax
import jax.numpy as jnp
from jax import lax
from jax.sharding import PartitionSpec as P

PASSK = 4


def pass_rate(correct, group_size):
    counts = group_size.astype(jnp.float32)
    hit_counts = correct.astype(jnp.float32)
    product = jnp.ones_like(counts)
    for offset in range(PASSK):
        product = product * (counts - hit_counts - offset) / (counts - offset)
    return 1.0 - product


def body(queries, key_rows, value_rows, cotangent, trace_ids, correct, group_size):
    tok_rows = queries.shape[0]
    half_rows = tok_rows // 2
    row_width = queries.shape[1]
    head_dim = key_rows.shape[1]
    head_count = row_width // head_dim
    ctx_count = lax.axis_size("ctx")
    my_index = lax.axis_index("ctx")
    length = tok_rows * ctx_count
    score_scale = 1.0 / math.sqrt(head_dim)
    pass_rates = pass_rate(correct, group_size)
    traces = jnp.arange(pass_rates.shape[0], dtype=jnp.int32)
    weights = jnp.sum(
        jnp.where(trace_ids[:, None] == traces[None, :], pass_rates[None, :], 0.0), axis=1
    )
    out_grads = (weights[:, None] * cotangent.astype(jnp.float32)).astype(jnp.bfloat16)
    first_base = my_index * tok_rows
    second_base = first_base + half_rows
    local_pos = jnp.arange(half_rows, dtype=jnp.int32)
    positions = jnp.concatenate([first_base + local_pos, second_base + local_pos], 0)
    last_first = first_base + half_rows - 1
    last_second = second_base + half_rows - 1
    query_all = queries.reshape(tok_rows, head_count, head_dim)
    grad_all = out_grads.reshape(tok_rows, head_count, head_dim)

    def run_block(running, key_block, value_block, key_start, block_fn):
        need_first = (key_start <= last_first).astype(jnp.int32)
        need_second = (key_start <= last_second).astype(jnp.int32)
        branch_index = need_first + 2 * need_second

        def skip_block(values_in):
            return values_in

        def first_only(values_in):
            return block_fn((0, half_rows), values_in, key_block, value_block, key_start)

        def second_only(values_in):
            return block_fn((half_rows, tok_rows), values_in, key_block, value_block, key_start)

        def both_halves(values_in):
            return block_fn((0, tok_rows), values_in, key_block, value_block, key_start)

        return lax.switch(branch_index, [skip_block, first_only, second_only, both_halves], running)

    def forward_block(row_span, running, key_block, value_block, key_start):
        row_begin, row_end = row_span
        row_peak, row_total, weighted = running
        query_part = query_all[row_begin:row_end]
        grad_part = grad_all[row_begin:row_end]
        query_pos = positions[row_begin:row_end]
        scores = (
            jnp.einsum("tqd,kd->tqk", query_part, key_block, preferred_element_type=jnp.float32)
            * score_scale
        )
        key_pos = key_start + jnp.arange(key_block.shape[0], dtype=jnp.int32)
        visible = key_pos[None, None, :] <= query_pos[:, None, None]
        block_peak = jnp.max(jnp.where(visible, scores, -1e30), axis=2)
        old_peak = row_peak[row_begin:row_end]
        new_peak = jnp.maximum(old_peak, block_peak)
        exp_terms = jnp.where(visible, jnp.exp(scores - new_peak[:, :, None]), 0.0)
        grad_probs = jnp.einsum(
            "tqd,kd->tqk", grad_part, value_block, preferred_element_type=jnp.float32
        )
        shrink = jnp.exp(old_peak - new_peak)
        new_total = row_total[row_begin:row_end] * shrink + jnp.sum(exp_terms, axis=2)
        new_weighted = weighted[row_begin:row_end] * shrink + jnp.sum(
            exp_terms * grad_probs, axis=2
        )
        return (
            row_peak.at[row_begin:row_end].set(new_peak),
            row_total.at[row_begin:row_end].set(new_total),
            weighted.at[row_begin:row_end].set(new_weighted),
        )

    row_peak = jnp.full((tok_rows, head_count), -1e30, jnp.float32)
    row_total = jnp.zeros((tok_rows, head_count), jnp.float32)
    weighted = jnp.zeros((tok_rows, head_count), jnp.float32)
    key_piece = lax.all_gather(key_rows, "ctx", axis=0, tiled=True)
    value_piece = lax.all_gather(value_rows, "ctx", axis=0, tiled=True)
    piece_rows = key_piece.shape[0]
    block_rows = math.gcd(piece_rows, 512)

    def forward_step(step_index, statistics):
        offset = step_index * block_rows
        key_block = lax.dynamic_slice_in_dim(key_piece, offset, block_rows, 0)
        value_block = lax.dynamic_slice_in_dim(value_piece, offset, block_rows, 0)
        return run_block(statistics, key_block, value_block, offset, forward_block)

    statistics = lax.fori_loop(
        0, piece_rows // block_rows, forward_step, (row_peak, row_total, weighted)
    )
    folded = statistics + (key_piece, value_piece)
    row_peak, row_total, weighted, key_store, value_store = folded
    log_totals = row_peak + jnp.log(row_total)
    delta_rows = weighted / row_total

    def backward_block(row_span, running, key_block, value_block, key_start):
        row_begin, row_end = row_span
        grad_query, zero_block = running
        query_part = query_all[row_begin:row_end]
        grad_part = grad_all[row_begin:row_end]
        query_pos = positions[row_begin:row_end]
        scores = (
            jnp.einsum("tqd,kd->tqk", query_part, key_block, preferred_element_type=jnp.float32)
            * score_scale
        )
        key_pos = key_start + jnp.arange(key_block.shape[0], dtype=jnp.int32)
        visible = key_pos[None, None, :] <= query_pos[:, None, None]
        probabilities = jnp.where(
            visible, jnp.exp(scores - log_totals[row_begin:row_end][:, :, None]), 0.0
        )
        prob_bf16 = probabilities.astype(jnp.bfloat16)
        grad_probs = jnp.einsum(
            "tqd,kd->tqk", grad_part, value_block, preferred_element_type=jnp.float32
        )
        grad_scores = (
            probabilities * (grad_probs - delta_rows[row_begin:row_end][:, :, None])
        ).astype(jnp.bfloat16)
        query_add = (
            jnp.einsum("tqk,kd->tqd", grad_scores, key_block, preferred_element_type=jnp.float32)
            * score_scale
        )
        key_add = (
            jnp.einsum("tqk,tqd->kd", grad_scores, query_part, preferred_element_type=jnp.float32)
            * score_scale
        )
        value_add = jnp.einsum(
            "tqk,tqd->kd", prob_bf16, grad_part, preferred_element_type=jnp.float32
        )
        return (
            grad_query.at[row_begin:row_end].add(query_add),
            jnp.concatenate([key_add, value_add], 1),
        )

    query_zero = jnp.zeros((tok_rows, head_count, head_dim), jnp.float32)
    key_block_rows = math.gcd(length, 512)

    def backward_step(step_index, running):
        grad_query, partial_sums = running
        key_start = step_index * key_block_rows
        key_block = lax.dynamic_slice_in_dim(key_store, key_start, key_block_rows, 0)
        value_block = lax.dynamic_slice_in_dim(value_store, key_start, key_block_rows, 0)
        zero_block = jnp.zeros((key_block_rows, 2 * head_dim), jnp.float32)
        grad_query, block_sums = run_block(
            (grad_query, zero_block), key_block, value_block, key_start, backward_block
        )
        partial_sums = lax.dynamic_update_slice_in_dim(partial_sums, block_sums, key_start, 0)
        return (grad_query, partial_sums)

    grad_query, partial_sums = lax.fori_loop(
        0,
        length // key_block_rows,
        backward_step,
        (query_zero, jnp.zeros((length, 2 * head_dim), jnp.float32)),
    )
    reduced = jnp.sum(
        lax.all_to_all(
            partial_sums.reshape(ctx_count, tok_rows, 2 * head_dim),
            "ctx",
            split_axis=0,
            concat_axis=0,
            tiled=True,
        ),
        axis=0,
    )
    grad_keys = reduced[:, :head_dim].astype(jnp.bfloat16)
    grad_values = reduced[:, head_dim:].astype(jnp.bfloat16)
    query_grads = grad_query.reshape(tok_rows, row_width)
    return (log_totals, query_grads, grad_keys, grad_values)


def solution(mesh):
    return jax.shard_map(
        body,
        mesh=mesh,
        in_specs=(
            P("ctx", "head"),
            P("ctx", "head"),
            P("ctx", "head"),
            P("ctx", "head"),
            P("ctx"),
            P(),
            P(),
        ),
        out_specs=(P("ctx", "head"), P("ctx", "head"), P("ctx", "head"), P("ctx", "head")),
        check_vma=False,
    )
```

profile of v0, /device:TPU:13, one launch (start us, length us, event | category | flops | bytes accessed | tf_op | source)
XLA Modules:
  0.0 124.0 jit_solution(4631487437105801853)
XLA Ops:
  0.7 0.7 fusion.61
  1.4 0.7 select_reduce_fusion.3
  2.1 1.0 multiply_convert_fusion.1
  3.1 0.2 copy.73
  3.3 0.2 copy.75
  3.5 1.1 copy.72
  4.6 0.2 copy.74
  4.8 17.1 %all_gather.6 = bf16[2048,128]{1,0:T(8,128)(2,1)S(1)} all-gather(bf16[128,128]{1,0:T(8,128)(2,1)S(1)} %copy-done.1), channel_id=1, replica_groups=mesh['ctx'=16,'head'=2] {'ctx'}, dimensions={0}, use_global_device_ids=true | all-gather | bytes 557056 | tf_op jit(solution)/shard_map/all_gather | solution.py:96
  21.9 22.8 %all_gather.7 = bf16[2048,128]{1,0:T(8,128)(2,1)S(1)} all-gather(bf16[128,128]{1,0:T(8,128)(2,1)S(1)} %copy-done.2), channel_id=1, replica_groups=mesh['ctx'=16,'head'=2] {'ctx'}, dimensions={0}, use_global_device_ids=true | all-gather | bytes 557056 | tf_op jit(solution)/shard_map/all_gather | solution.py:97
  44.8 3.9 %while.53 = (s32[]{:T(128)}, f32[128,6]{0,1:T(8,128)S(1)}, f32[128,6]{0,1:T(8,128)S(1)}, f32[128,6]{0,1:T(8,128)S(1)}, s32[]{:T(128)}, /*index=5*/s32[]{:T(128)}...) while((s32[]{:T(128)}, f32[128,6]{0,1:T(8,128)S(1)}, ...), condition=%wide.region_15.0_spmd.clone, body=%wide.region_1.15_spmd.clone.sunk | while | flops 205327120 | bytes 6221379 | solution.py:107
  44.8 1.7 %conditional.6 = ((f32[128,6]{0,1:T(8,128)S(1)}, f32[128,6]{0,1:T(8,128)S(1)}, f32[128,6]{0,1:T(8,128)S(1)})) conditional(s32[]{:T(128)} %clamp.18, (f32[128,6]{0,1:T(8,128)S(1)}, f32[128,6]{0,1:T(8,128)S(1)}, f32[128,6]{0,1:T(8,128)S(1)}) %tuple.202, (f32[128,6]{0,1:T(8,128)S(1)}, s32[]{:T(128)}, s32[]{:T(128)}, ...), branch_computations={%region_2.2_spmd, %region_3.6_spmd, %region_7.10_spmd, %region_11.... | conditional | flops 205327104 | bytes 5696036 | solution.py:61
  44.9 0.1 broadcast_compare_fusion.2
  45.0 0.5 select_reduce_fusion.2
  45.4 0.6 multiply_reduce_fusion
  46.0 0.5 fusion.20
  46.6 1.7 %conditional.6 = ((f32[128,6]{0,1:T(8,128)S(1)}, f32[128,6]{0,1:T(8,128)S(1)}, f32[128,6]{0,1:T(8,128)S(1)})) conditional(s32[]{:T(128)} %clamp.18, (f32[128,6]{0,1:T(8,128)S(1)}, f32[128,6]{0,1:T(8,128)S(1)}, f32[128,6]{0,1:T(8,128)S(1)}) %tuple.202, (f32[128,6]{0,1:T(8,128)S(1)}, s32[]{:T(128)}, s32[]{:T(128)}, ...), branch_computations={%region_2.2_spmd, %region_3.6_spmd, %region_7.10_spmd, %region_11.... | conditional | flops 205327104 | bytes 5696036 | solution.py:61
  46.8 0.5 select_reduce_fusion.2
  47.3 0.6 multiply_reduce_fusion
  47.8 0.5 fusion.20
  48.7 1.5 %broadcast_in_dim.124.clone = f32[2048,256]{1,0:T(8,128)} broadcast(f32[]{:T(128)} %constant.488.clone.1), dimensions={} | broadcast | bytes 2097156 | tf_op jit(solution)/shard_map/broadcast_in_dim | solution.py:172
  50.2 8.7 %while.54 = (s32[]{:T(128)}, f32[128,6,128]{2,0,1:T(8,128)S(1)}, f32[2048,256]{1,0:T(8,128)}, s32[]{:T(128)}, s32[]{:T(128)}, /*index=5*/bf16[2048,128]{1,0:T(8,...) while((s32[]{:T(128)}, f32[128,6,128]{2,0,1:T(8,128)S(1)}, ...), condition=%wide.region_21.22_spmd.clone, body=%wide.region_16.21_spmd.clone.sunk | while | flops 506528256 | bytes 13381159 | solution.py:168
  50.2 2.1 %conditional.7 = (f32[128,6,128]{2,0,1:T(8,128)S(1)}, f32[512,256]{0,1:T(8,128)S(1)}) conditional(s32[]{:T(128)} %clamp.19, f32[128,6,128]{2,0,1:T(8,128)S(1)} %get-tuple-element.1421, (f32[128,6,128]{2,0,1:T(8,128)S(1)}, s32[]{:T(128)}, s32[]{:T(128)}, bf16[128,6,128]{0,2,1:T(8,128)(2,1)S(1)}, ...), branch_computations={%region_17.17_spmd, %region_18.18_spmd, %region_19.19_spmd, %regio... | conditional | flops 506528256 | bytes 10758676 | solution.py:61
  50.4 0.5 exponential_select_fusion.3
  50.9 0.3 convolution_bitcast_fusion.4
  51.2 0.4 multiply_convert_fusion
  51.6 0.3 fusion.56
  51.9 0.4 fusion.55
  52.3 0.2 copy.91
  52.5 0.8 constant_dynamic-update-slice_fusion.2
  53.4 2.1 %conditional.7 = (f32[128,6,128]{2,0,1:T(8,128)S(1)}, f32[512,256]{0,1:T(8,128)S(1)}) conditional(s32[]{:T(128)} %clamp.19, f32[128,6,128]{2,0,1:T(8,128)S(1)} %get-tuple-element.1421, (f32[128,6,128]{2,0,1:T(8,128)S(1)}, s32[]{:T(128)}, s32[]{:T(128)}, bf16[128,6,128]{0,2,1:T(8,128)(2,1)S(1)}, ...), branch_computations={%region_17.17_spmd, %region_18.18_spmd, %region_19.19_spmd, %regio... | conditional | flops 506528256 | bytes 10758676 | solution.py:61
  53.5 0.5 exponential_select_fusion.3
  54.1 0.3 convolution_bitcast_fusion.4
  54.3 0.4 multiply_convert_fusion
  54.8 0.3 fusion.56
  55.0 0.4 fusion.55
  55.5 0.2 copy.91
  55.7 0.9 constant_dynamic-update-slice_fusion.2
  56.7 0.2 copy.91
  56.9 0.9 constant_dynamic-update-slice_fusion.2
  57.8 0.2 copy.91
  58.1 0.9 constant_dynamic-update-slice_fusion.2
  58.9 2.9 %copy.78 = f32[16,128,256]{1,2,0:T(8,128)} copy(f32[16,128,256]{2,1,0:T(8,128)} %bitcast.88) | data formatting | bytes 4194304 | tf_op jit(solution)/shard_map/reshape | solution.py:176
  61.8 13.2 %all-to-all-start = ((f32[16,128,256]{1,2,0:T(8,128)}), f32[16,128,256]{1,2,0:T(8,128)S(1)}, u32[]{:S(2)}, u32[]{:S(2)}) async-start(f32[16,128,256]{1,2,0:T(8,128)} %copy.78), calls=%async_computation | async-start | bytes 4194304 | tf_op jit(solution)/shard_map/all_to_all | solution.py:175
  75.0 0.2 copy.76
  75.2 0.9 copy.80
  76.1 46.3 %all-to-all-done = f32[16,128,256]{1,2,0:T(8,128)S(1)} async-done(((f32[16,128,256]{1,2,0:T(8,128)}), f32[16,128,256]{1,2,0:T(8,128)S(1)}, u32[]{:S(2)}, u32[]{:S(2)}) %all-to-all-start) | async-done | bytes 2097184 | tf_op jit(solution)/shard_map/all_to_all | solution.py:175
  122.5 0.7 copy.82
  123.2 0.7 copy.81
  (60 shorter events, 1.3 us)
Async XLA Ops:
  0.6 4.1 %copy-start.1 = (bf16[128,128]{1,0:T(8,128)(2,1)S(1)}, bf16[128,128]{1,0:T(8,128)(2,1)}, u32[]{:S(2)}) copy-start(bf16[128,128]{1,0:T(8,128)(2,1)} %param.52) | copy-start | bytes 98308
  0.6 21.2 %copy-start.2 = (bf16[128,128]{1,0:T(8,128)(2,1)S(1)}, bf16[128,128]{1,0:T(8,128)(2,1)}, u32[]{:S(2)}) copy-start(bf16[128,128]{1,0:T(8,128)(2,1)} %param.53) | copy-start | bytes 98308
  58.9 2.9 %copy-start = (f32[128,6]{0,1:T(8,128)}, f32[128,6]{0,1:T(8,128)S(1)}, u32[]{:S(2)}) copy-start(f32[128,6]{0,1:T(8,128)S(1)} %get-tuple-element.1469) | copy-start | bytes 9220
  61.8 60.6 %all-to-all-start = ((f32[16,128,256]{1,2,0:T(8,128)}), f32[16,128,256]{1,2,0:T(8,128)S(1)}, u32[]{:S(2)}, u32[]{:S(2)}) async-start(f32[16,128,256]{1,2,0:T(8,128)} %copy.78), calls=%async_computation | async-start | bytes 4194304 | tf_op jit(solution)/shard_map/all_to_all | solution.py:175
where the time goes:
time: 124 us
  waiting for transfers between devices  46.3 us (37%)
  blocking collectives  39.9 us (32%)
  starting transfers between devices  13.2 us (11%)
  local copies, waits for them, and re-layouts  13.1 us (11%)
  matrix products  5.79 us (5%)
  other arithmetic  4.14 us (3%)
    all_to_all x1, waiting for transfers between devices, body(): lax.all_to_all(partial_sums.reshape(ctx_count, tok_rows, 2 * head_dim), '...  46.3 us
    all_gather x1, blocking collectives, body(): value_piece = lax.all_gather(value_rows, 'ctx', axis=0, tiled=True)  22.8 us
    all_gather x1, blocking collectives, body(): key_piece = lax.all_gather(key_rows, 'ctx', axis=0, tiled=True)  17.1 us
    all_to_all x1, starting transfers between devices, body(): lax.all_to_all(partial_sums.reshape(ctx_count, tok_rows, 2 * head_dim), '...  13.2 us
    dynamic_update_slice x8, local copies, waits for them, and re-layouts, backward_step(): lax.dynamic_update_slice_in_dim(partial_sums, block_sums, key_start, 0)  4.17 us
    unnamed x12, local copies, waits for them, and re-layouts  3.83 us
    reshape x1, local copies, waits for them, and re-layouts, body(): partial_sums.reshape(ctx_count, tok_rows, 2 * head_dim)  2.89 us
  transfers between devices with their start and end apart: 1, of which 1 were waited for; matrix products, arithmetic and copies ran while one was open for 1% of the time, Pallas kernels for 0%

commit v1 on v0

--- a/solution.py
+++ b/solution.py
@@ -5,6 +5,18 @@
 from jax.sharding import PartitionSpec as P
 
 PASSK = 4
+
+
+def collect(x, axis, dim):
+    ways, here = (lax.axis_size(axis), lax.axis_index(axis))
+    grown, reach = (x, 1)
+    while reach < ways:
+        theirs = lax.ppermute(grown, axis, [(d, d ^ reach) for d in range(ways)])
+        mine_first = jnp.concatenate([grown, theirs], axis=dim)
+        theirs_first = jnp.concatenate([theirs, grown], axis=dim)
+        grown = jnp.where(here & reach == 0, mine_first, theirs_first)
+        reach = 2 * reach
+    return grown
 
 
 def pass_rate(correct, group_size):
@@ -94,7 +106,7 @@
     row_total = jnp.zeros((tok_rows, head_count), jnp.float32)
     weighted = jnp.zeros((tok_rows, head_count), jnp.float32)
     key_piece = lax.all_gather(key_rows, "ctx", axis=0, tiled=True)
-    value_piece = lax.all_gather(value_rows, "ctx", axis=0, tiled=True)
+    value_piece = collect(value_rows, "ctx", 0)
     piece_rows = key_piece.shape[0]
     block_rows = math.gcd(piece_rows, 512)
 

time: 124 us -> 117 us (0.944)
  blocking collectives: 39.9 us -> 23.8 us
  waiting for transfers between devices: 46.3 us -> 51.5 us
  starting transfers between devices: 13.2 us -> 15.9 us
    all_gather x1 -> x0, blocking collectives: 22.8 us -> none  [body(): value_piece = lax.all_gather(value_rows, 'ctx', axis=0, tiled=True)]
    all_gather x1, blocking collectives: 17.1 us -> 23.8 us  [body(): key_piece = lax.all_gather(key_rows, 'ctx', axis=0, tiled=True)]
    ppermute x0 -> x4, waiting for transfers between devices: none -> 5.13 us  [collect(): theirs = lax.ppermute(grown, axis, [(d, d ^ reach) for d in range(ways)])]
    ppermute x0 -> x4, starting transfers between devices: none -> 3.64 us  [collect(): theirs = lax.ppermute(grown, axis, [(d, d ^ reach) for d in range(ways)])]
  transfers between devices with their start and end apart: 1 -> 5, of which waited for: 1 -> 4; matrix products, arithmetic and copies ran while one was open for 1% -> 4% of each run, Pallas kernels for 0% -> 0%
where the time goes in v1:
time: 117 us; the launch traced here: 116 us
  waiting for transfers between devices  51.5 us (44%)
  blocking collectives  23.8 us (20%)
  starting transfers between devices  15.9 us (14%)
  local copies, waits for them, and re-layouts  12.1 us (10%)
  matrix products  5.79 us (5%)
  other arithmetic  5.23 us (4%)
    all_to_all x1, waiting for transfers between devices, body(): lax.all_to_all(partial_sums.reshape(ctx_count, tok_rows, 2 * head_dim), '...  46.3 us
    all_gather x1, blocking collectives, body(): key_piece = lax.all_gather(key_rows, 'ctx', axis=0, tiled=True)  23.8 us
    all_to_all x1, starting transfers between devices, body(): lax.all_to_all(partial_sums.reshape(ctx_count, tok_rows, 2 * head_dim), '...  12.3 us
    ppermute x4, waiting for transfers between devices, collect(): theirs = lax.ppermute(grown, axis, [(d, d ^ reach) for d in range(ways)])  5.13 us
    dynamic_update_slice x8, local copies, waits for them, and re-layouts, backward_step(): lax.dynamic_update_slice_in_dim(partial_sums, block_sums, key_start, 0)  4.17 us
    ppermute x4, starting transfers between devices, collect(): theirs = lax.ppermute(grown, axis, [(d, d ^ reach) for d in range(ways)])  3.64 us
    unnamed x12, local copies, waits for them, and re-layouts  2.89 us
    reshape x1, local copies, waits for them, and re-layouts, body(): partial_sums.reshape(ctx_count, tok_rows, 2 * head_dim)  2.89 us
  transfers between devices with their start and end apart: 5, of which 4 were waited for; matrix products, arithmetic and copies ran while one was open for 4% of the time, Pallas kernels for 0%

profile of v1, /device:TPU:13, one launch (start us, length us, event | category | flops | bytes accessed | tf_op | source)
XLA Modules:
  0.0 116.0 jit_solution(1207560581426372436)
XLA Ops:
  0.7 0.7 collective-permute-start
  1.4 0.7 fusion.61
  2.1 0.4 collective-permute-done
  2.5 0.9 maximum_select_fusion.3
  3.3 0.3 collective-permute-start.1
  3.6 0.7 select_reduce_fusion.3
  4.4 2.1 %collective-permute-done.1 = bf16[256,128]{1,0:T(8,128)(2,1)S(1)} collective-permute-done((bf16[256,128]{1,0:T(8,128)(2,1)S(1)}, bf16[256,128]{1,0:T(8,128)(2,1)S(1)}, u32[]{:S(2)}, u32[]{:S(2)}) %collective-permute-start.1) | collective-permute-done | bytes 65568 | tf_op jit(solution)/shard_map/ppermute | solution.py:14
  6.5 0.2 collective-permute-start.2
  6.8 1.0 multiply_convert_fusion.1
  7.8 2.6 %collective-permute-done.2 = bf16[512,128]{1,0:T(8,128)(2,1)S(1)} collective-permute-done((bf16[512,128]{1,0:T(8,128)(2,1)S(1)}, bf16[512,128]{1,0:T(8,128)(2,1)S(1)}, u32[]{:S(2)}, u32[]{:S(2)}) %collective-permute-start.2) | collective-permute-done | bytes 131104 | tf_op jit(solution)/shard_map/ppermute | solution.py:14
  10.5 2.4 %collective-permute-start.3 = (bf16[1024,128]{1,0:T(8,128)(2,1)S(1)}, bf16[1024,128]{1,0:T(8,128)(2,1)S(1)}, u32[]{:S(2)}, u32[]{:S(2)}) collective-permute-start(bf16[1024,128]{1,0:T(8,128)(2,1)S(1)} %maximum_select_fusion.1), channel_id=1, source_target_pairs={{0,16},{2,18},{4,20},{6,22},{8,24},{10,26},{12,28},{14,30},{16,0},... | collective-permute-start | bytes 786440 | tf_op jit(solution)/shard_map/ppermute | solution.py:14
  13.7 23.8 %all_gather.3 = bf16[2048,128]{1,0:T(8,128)(2,1)S(1)} all-gather(bf16[128,128]{1,0:T(8,128)(2,1)S(1)} %copy-done.2), channel_id=1, replica_groups=mesh['ctx'=16,'head'=2] {'ctx'}, dimensions={0}, use_global_device_ids=true | all-gather | bytes 557056 | tf_op jit(solution)/shard_map/all_gather | solution.py:108
  37.6 3.9 %while.53 = (s32[]{:T(128)}, f32[128,6]{0,1:T(8,128)S(1)}, f32[128,6]{0,1:T(8,128)S(1)}, f32[128,6]{0,1:T(8,128)S(1)}, s32[]{:T(128)}, /*index=5*/s32[]{:T(128)}...) while((s32[]{:T(128)}, f32[128,6]{0,1:T(8,128)S(1)}, ...), condition=%wide.region_15.16_spmd.clone, body=%wide.region_1.15_spmd.clone.sunk | while | flops 205327120 | bytes 6221379 | solution.py:119
  37.7 1.7 %conditional.6 = ((f32[128,6]{0,1:T(8,128)S(1)}, f32[128,6]{0,1:T(8,128)S(1)}, f32[128,6]{0,1:T(8,128)S(1)})) conditional(s32[]{:T(128)} %clamp.18, (f32[128,6]{0,1:T(8,128)S(1)}, f32[128,6]{0,1:T(8,128)S(1)}, f32[128,6]{0,1:T(8,128)S(1)}) %tuple.202, (f32[128,6]{0,1:T(8,128)S(1)}, s32[]{:T(128)}, s32[]{:T(128)}, ...), branch_computations={%region_2.2_spmd, %region_3.6_spmd, %region_7.10_spmd, %region_11.... | conditional | flops 205327104 | bytes 5696036 | solution.py:73
  37.9 0.5 select_reduce_fusion.2
  38.3 0.6 multiply_reduce_fusion
  38.9 0.5 fusion.20
  39.5 1.7 %conditional.6 = ((f32[128,6]{0,1:T(8,128)S(1)}, f32[128,6]{0,1:T(8,128)S(1)}, f32[128,6]{0,1:T(8,128)S(1)})) conditional(s32[]{:T(128)} %clamp.18, (f32[128,6]{0,1:T(8,128)S(1)}, f32[128,6]{0,1:T(8,128)S(1)}, f32[128,6]{0,1:T(8,128)S(1)}) %tuple.202, (f32[128,6]{0,1:T(8,128)S(1)}, s32[]{:T(128)}, s32[]{:T(128)}, ...), branch_computations={%region_2.2_spmd, %region_3.6_spmd, %region_7.10_spmd, %region_11.... | conditional | flops 205327104 | bytes 5696036 | solution.py:73
  39.7 0.5 select_reduce_fusion.2
  40.2 0.6 multiply_reduce_fusion
  40.7 0.5 fusion.20
  41.6 1.5 %broadcast_in_dim.124.clone = f32[2048,256]{1,0:T(8,128)} broadcast(f32[]{:T(128)} %constant.491.clone.1), dimensions={} | broadcast | bytes 2097156 | tf_op jit(solution)/shard_map/broadcast_in_dim | solution.py:184
  43.1 8.7 %while.54 = (s32[]{:T(128)}, f32[128,6,128]{2,0,1:T(8,128)S(1)}, f32[2048,256]{1,0:T(8,128)}, s32[]{:T(128)}, s32[]{:T(128)}, /*index=5*/bf16[2048,128]{1,0:T(8,...) while((s32[]{:T(128)}, f32[128,6,128]{2,0,1:T(8,128)S(1)}, ...), condition=%wide.region_21.22_spmd.clone, body=%wide.region_16.0_spmd.clone.sunk | while | flops 506528256 | bytes 13381159 | solution.py:180
  43.1 2.1 %conditional.7 = (f32[128,6,128]{2,0,1:T(8,128)S(1)}, f32[512,256]{0,1:T(8,128)S(1)}) conditional(s32[]{:T(128)} %clamp.19, f32[128,6,128]{2,0,1:T(8,128)S(1)} %get-tuple-element.1421, (f32[128,6,128]{2,0,1:T(8,128)S(1)}, s32[]{:T(128)}, s32[]{:T(128)}, bf16[128,6,128]{0,2,1:T(8,128)(2,1)S(1)}, ...), branch_computations={%region_17.17_spmd, %region_18.18_spmd, %region_19.19_spmd, %regio... | conditional | flops 506528256 | bytes 10758676 | solution.py:73
  43.2 0.5 exponential_select_fusion.3
  43.8 0.3 convolution_bitcast_fusion.4
  44.1 0.4 multiply_convert_fusion
  44.5 0.3 fusion.56
  44.7 0.4 fusion.55
  45.2 0.2 copy.91
  45.4 0.8 constant_dynamic-update-slice_fusion.2
  46.3 2.1 %conditional.7 = (f32[128,6,128]{2,0,1:T(8,128)S(1)}, f32[512,256]{0,1:T(8,128)S(1)}) conditional(s32[]{:T(128)} %clamp.19, f32[128,6,128]{2,0,1:T(8,128)S(1)} %get-tuple-element.1421, (f32[128,6,128]{2,0,1:T(8,128)S(1)}, s32[]{:T(128)}, s32[]{:T(128)}, bf16[128,6,128]{0,2,1:T(8,128)(2,1)S(1)}, ...), branch_computations={%region_17.17_spmd, %region_18.18_spmd, %region_19.19_spmd, %regio... | conditional | flops 506528256 | bytes 10758676 | solution.py:73
  46.4 0.5 exponential_select_fusion.3
  47.0 0.3 convolution_bitcast_fusion.4
  47.2 0.4 multiply_convert_fusion
  47.6 0.3 fusion.56
  47.9 0.4 fusion.55
  48.4 0.2 copy.91
  48.6 0.9 constant_dynamic-update-slice_fusion.2
  49.7 0.9 constant_dynamic-update-slice_fusion.2
  50.7 0.2 copy.91
  50.9 0.9 constant_dynamic-update-slice_fusion.2
  51.8 2.9 %copy.78 = f32[16,128,256]{1,2,0:T(8,128)} copy(f32[16,128,256]{2,1,0:T(8,128)} %bitcast.88) | data formatting | bytes 4194304 | tf_op jit(solution)/shard_map/reshape | solution.py:188
  54.7 12.3 %all-to-all-start = ((f32[16,128,256]{1,2,0:T(8,128)}), f32[16,128,256]{1,2,0:T(8,128)S(1)}, u32[]{:S(2)}, u32[]{:S(2)}) async-start(f32[16,128,256]{1,2,0:T(8,128)} %copy.78), calls=%async_computation | async-start | bytes 4194304 | tf_op jit(solution)/shard_map/all_to_all | solution.py:187
  67.1 0.9 copy.80
  68.1 46.3 %all-to-all-done = f32[16,128,256]{1,2,0:T(8,128)S(1)} async-done(((f32[16,128,256]{1,2,0:T(8,128)}), f32[16,128,256]{1,2,0:T(8,128)S(1)}, u32[]{:S(2)}, u32[]{:S(2)}) %all-to-all-start) | async-done | bytes 2097184 | tf_op jit(solution)/shard_map/all_to_all | solution.py:187
  114.5 0.7 copy.82
  115.2 0.7 copy.81
  (71 shorter events, 2.7 us)
Async XLA Ops:
  0.6 12.7 %copy-start = (bf16[128,768]{1,0:T(8,128)(2,1)S(1)}, bf16[128,768]{1,0:T(8,128)(2,1)}, u32[]{:S(2)}) copy-start(bf16[128,768]{1,0:T(8,128)(2,1)} %param.51) | copy-start | bytes 589828
  0.6 13.0 %copy-start.2 = (bf16[128,128]{1,0:T(8,128)(2,1)S(1)}, bf16[128,128]{1,0:T(8,128)(2,1)}, u32[]{:S(2)}) copy-start(bf16[128,128]{1,0:T(8,128)(2,1)} %param.52) | copy-start | bytes 98308
  0.7 1.8 %collective-permute-start = (bf16[128,128]{1,0:T(8,128)(2,1)}, bf16[128,128]{1,0:T(8,128)(2,1)S(1)}, u32[]{:S(2)}, u32[]{:S(2)}) collective-permute-start(bf16[128,128]{1,0:T(8,128)(2,1)} %param.53), channel_id=1, source_target_pairs={{0,2},{2,0},{4,6},{6,4},{8,10},{10,8},{12,14},{14,12},{16,18},{18,... | collective-permute-start | bytes 98312 | tf_op jit(solution)/shard_map/ppermute | solution.py:14
  3.3 3.2 %collective-permute-start.1 = (bf16[256,128]{1,0:T(8,128)(2,1)S(1)}, bf16[256,128]{1,0:T(8,128)(2,1)S(1)}, u32[]{:S(2)}, u32[]{:S(2)}) collective-permute-start(bf16[256,128]{1,0:T(8,128)(2,1)S(1)} %maximum_select_fusion.3), channel_id=1, source_target_pairs={{0,4},{2,6},{4,0},{6,2},{8,12},{10,14},{12,8},{14,10},{16,20},{18,... | collective-permute-start | bytes 196616 | tf_op jit(solution)/shard_map/ppermute | solution.py:14
  6.5 3.9 %collective-permute-start.2 = (bf16[512,128]{1,0:T(8,128)(2,1)S(1)}, bf16[512,128]{1,0:T(8,128)(2,1)S(1)}, u32[]{:S(2)}, u32[]{:S(2)}) collective-permute-start(bf16[512,128]{1,0:T(8,128)(2,1)S(1)} %maximum_select_fusion.2), channel_id=1, source_target_pairs={{0,8},{2,10},{4,12},{6,14},{8,0},{10,2},{12,4},{14,6},{16,24},{18,... | collective-permute-start | bytes 393224 | tf_op jit(solution)/shard_map/ppermute | solution.py:14
  10.5 26.9 %collective-permute-start.3 = (bf16[1024,128]{1,0:T(8,128)(2,1)S(1)}, bf16[1024,128]{1,0:T(8,128)(2,1)S(1)}, u32[]{:S(2)}, u32[]{:S(2)}) collective-permute-start(bf16[1024,128]{1,0:T(8,128)(2,1)S(1)} %maximum_select_fusion.1), channel_id=1, source_target_pairs={{0,16},{2,18},{4,20},{6,22},{8,24},{10,26},{12,28},{14,30},{16,0},... | collective-permute-start | bytes 786440 | tf_op jit(solution)/shard_map/ppermute | solution.py:14
  51.8 2.9 %copy-start.1 = (f32[128,6]{0,1:T(8,128)}, f32[128,6]{0,1:T(8,128)S(1)}, u32[]{:S(2)}) copy-start(f32[128,6]{0,1:T(8,128)S(1)} %get-tuple-element.1473) | copy-start | bytes 9220
  54.7 59.7 %all-to-all-start = ((f32[16,128,256]{1,2,0:T(8,128)}), f32[16,128,256]{1,2,0:T(8,128)S(1)}, u32[]{:S(2)}, u32[]{:S(2)}) async-start(f32[16,128,256]{1,2,0:T(8,128)} %copy.78), calls=%async_computation | async-start | bytes 4194304 | tf_op jit(solution)/shard_map/all_to_all | solution.py:187
